TPU v7x, 512 devices: a whole 4x8x8 slice. The times are simulated.
512 devices in a mesh: op: 16 (over y_lo, z), bond: 32 (over y_hi, x, core).
Axes of the slice: x: 4, y: 8 (y_hi: 4, y_lo: 2; y = y_hi * 2 + y_lo), z: 8, core: 2. Of those that a mesh axis runs over, the one named last changes fastest.
Arguments:
- vectors: bfloat16 [2, 64, 256, 256], P(None, 'bond'), may hold values from -6 to 6
- left_ops: bfloat16 [128, 64, 256, 256], P('op', 'bond'), may hold values from -0.03125 to 0.03125
- right_ops: bfloat16 [128, 64, 256, 256], P('op', 'bond'), may hold values from -0.375 to 0.375
- block_sizes: int32 [64, 2], P('bond'), may hold values from 32 to 256, as said below
- term_shifts: int32 [128], P('op'), may hold values from -1 to 1
Outputs:
- sigma: float32 [2, 64, 256, 256], P(None, 'bond', 'op')
Inputs may be any that keep to these rules, and one draw needn't show every extreme that they name: `block_sizes`: some block has both live dimensions 256 and some other block both 256 // 8.
All inputs are finite; a program needn't handle non-finite values.
Results may differ from a plain program's by a relative error of at most 0.0029.
Values may be sent and summed in bfloat16 or wider, within the bound.
No kernel may reach another device: no remote copies, remote signals or barrier semaphores. Data moves between devices by JAX's collectives and lax.ppermute only.
A program may use at most 64 MiB of HBM per device.

v0:
```python
import jax
import jax.numpy as jnp
from jax import lax
from jax.sharding import PartitionSpec as P


def extended(cells, sides, width):
    for axis, dim in sides:
        count = lax.axis_size(axis)
        ends = count - 1
        head = lax.slice_in_dim(cells, 0, width, axis=dim)
        tail = lax.slice_in_dim(cells, cells.shape[dim] - width, cells.shape[dim], axis=dim)
        cells = jnp.concatenate(
            [
                lax.ppermute(tail, axis, [(i, (i + 1) % count) for i in range(ends)]),
                cells,
                lax.ppermute(head, axis, [((i + 1) % count, i) for i in range(ends)]),
            ],
            axis=dim,
        )
    return cells


def per_device(vectors, left_ops, right_ops, block_sizes, term_shifts):
    block_count = vectors.shape[1]
    block_order = vectors.shape[2]
    row_index = jnp.arange(block_order, dtype=jnp.int32)
    live_mask = (row_index[None, :, None] < block_sizes[:, 0][:, None, None]) & (
        row_index[None, None, :] < block_sizes[:, 1][:, None, None]
    )
    masked = jnp.where(live_mask[None], vectors, jnp.zeros((), vectors.dtype))
    padded = extended(masked, (("bond", 1),), 1)

    def add_term(accumulated, operands):
        left_block, right_block, term_shift = operands
        start_block = 1 - term_shift
        source_blocks = lax.dynamic_slice_in_dim(padded, start_block, block_count, 1)
        half_product = jnp.einsum(
            "bik,vbkj->vbij", left_block, source_blocks, preferred_element_type=jnp.float32
        ).astype(jnp.bfloat16)
        term_value = jnp.einsum(
            "vbij,blj->vbil", half_product, right_block, preferred_element_type=jnp.float32
        )
        return (accumulated + term_value, None)

    initial = jnp.zeros((vectors.shape[0], block_count, block_order, block_order), jnp.float32)
    accumulated, _ = lax.scan(add_term, initial, (left_ops, right_ops, term_shifts))
    op_count = lax.axis_size("op")
    share_rows = block_order // op_count
    first_row = lax.axis_index("op") * share_rows
    summed = lax.psum(accumulated, "op")
    own_share = lax.dynamic_slice_in_dim(summed, first_row, share_rows, 2)
    live_share = lax.dynamic_slice_in_dim(live_mask, first_row, share_rows, 1)
    return jnp.where(live_share[None], own_share, jnp.zeros((), own_share.dtype))


def solution(mesh):
    in_specs = (
        P(None, "bond", None, None),
        P("op", "bond", None, None),
        P("op", "bond", None, None),
        P("bond", None),
        P("op"),
    )
    out_specs = P(None, "bond", "op", None)
    return jax.shard_map(
        per_device, mesh=mesh, in_specs=in_specs, out_specs=out_specs, check_vma=False
    )
```

profile of v0, /device:TPU:2, one launch (start us, length us, event | category | flops | bytes accessed | tf_op | source)
XLA Modules:
  0.0 213.6 jit_solution(7319213809346613324)
XLA Ops:
  6.5 0.0 all-reduce.2.cloned.1.call-start
  6.5 1.0 slice_reduce_fusion.1
  7.5 0.1 iota_compare_fusion
  7.6 0.1 broadcast_and_fusion
  7.7 0.0 copy-start
  7.7 1.1 broadcast_select_fusion
  8.9 1.9 collective-permute-start
  10.8 3.6 %collective-permute-start.1 = (bf16[2,1,256,256]{3,2,1,0:T(8,128)(2,1)S(1)}, bf16[2,1,256,256]{3,2,1,0:T(8,128)(2,1)S(1)}, u32[]{:S(2)}, u32[]{:S(2)}) collective-permute-start(bf16[2,1,256,256]{3,2,1,0:T(8,128)(2,1)S(1)} %get-tuple-element.119), channel_id=1, source_target_pairs={{1,0},{2,1},{3,2},{4,3},{5,4},{6,5},{7,6},{8,7},{9,8},{10,9},{11,1... | collective-permute-start | bytes 786440 | tf_op jit(solution)/shard_map/ppermute | solution.py:17
  14.5 2.1 collective-permute-done
  16.6 1.8 collective-permute-done.1
  18.3 0.1 pad_maximum_fusion
  18.5 0.0 copy-done
  18.5 29.0 %while.13 = (s32[]{:T(128)}, f32[2,2,256,256]{2,3,0,1:T(8,128)S(1)}, bf16[8,2,256,256]{3,2,1,0:T(8,128)(2,1)}, s32[8]{0:T(128)S(1)}, bf16[2,4,256,256]{3,2,1,0:T...) while((s32[]{:T(128)}, ...), condition=%wide.region_1.2_spmd.clone, body=%wide.region_0.1_spmd.clone.sunk | while | flops 269221888 | bytes 3147952 | solution.py:47
  18.5 0.7 dynamic_slice.60
  20.4 1.7 fusion.20
  22.1 0.7 dynamic_slice.60
  24.0 1.7 fusion.20
  25.7 0.7 dynamic_slice.60
  27.7 1.7 fusion.20
  29.4 0.7 dynamic_slice.60
  31.3 1.7 fusion.20
  33.0 0.7 dynamic_slice.60
  34.9 1.7 fusion.20
  36.6 0.7 dynamic_slice.60
  38.5 1.7 fusion.20
  40.2 0.7 dynamic_slice.60
  42.2 1.7 fusion.20
  43.9 0.7 dynamic_slice.60
  45.8 1.7 fusion.20
  47.5 1.4 copy.6
  48.9 0.0 all-reduce.2.cloned.1.call-update
  48.9 156.4 %all-reduce.2.cloned.1.call-done = f32[2,2,256,256]{3,2,1,0:T(8,128)} async-done(((f32[2,2,256,256]{3,2,1,0:T(8,128)}), f32[2,2,256,256]{3,2,1,0:T(8,128)}) %all-reduce.2.cloned.1.call-update) | async-done | bytes 1048592 | tf_op jit(solution)/shard_map/psum | solution.py:51
  205.3 1.5 dynamic-slice_select_fusion
  (3 shorter events, 0.0 us)
Async XLA Ops:
  6.5 198.7 %all-reduce.2.cloned.1.call-start = ((), (), s32[]{:S(2)}) async-start(), calls=%async_computation | async-start | bytes 2097152 | tf_op jit(solution)/shard_map/psum | solution.py:51
  7.7 10.7 %copy-start = (s32[8]{0:T(128)S(1)}, s32[8]{0:T(128)}, u32[]{:S(2)}) copy-start(s32[8]{0:T(128)} %param.11) | copy-start | bytes 100
  8.9 7.7 %collective-permute-start = (bf16[2,1,256,256]{3,2,1,0:T(8,128)(2,1)S(1)}, bf16[2,1,256,256]{3,2,1,0:T(8,128)(2,1)S(1)}, u32[]{:S(2)}, u32[]{:S(2)}) collective-permute-start(bf16[2,1,256,256]{3,2,1,0:T(8,128)(2,1)S(1)} %get-tuple-element.118), channel_id=1, source_target_pairs={{0,1},{1,2},{2,3},{3,4},{4,5},{5,6},{6,7},{7,8},{8,9},{9,10},{10,1... | collective-permute-start | bytes 786440 | tf_op jit(solution)/shard_map/ppermute | solution.py:15
  10.8 7.5 %collective-permute-start.1 = (bf16[2,1,256,256]{3,2,1,0:T(8,128)(2,1)S(1)}, bf16[2,1,256,256]{3,2,1,0:T(8,128)(2,1)S(1)}, u32[]{:S(2)}, u32[]{:S(2)}) collective-permute-start(bf16[2,1,256,256]{3,2,1,0:T(8,128)(2,1)S(1)} %get-tuple-element.119), channel_id=1, source_target_pairs={{1,0},{2,1},{3,2},{4,3},{5,4},{6,5},{7,6},{8,7},{9,8},{10,9},{11,1... | collective-permute-start | bytes 786440 | tf_op jit(solution)/shard_map/ppermute | solution.py:17
Sparse Core Ops, SparseCore 0:
  49.0 156.2 all-reduce.1
where the time goes:
time: 214 us
  waiting for transfers between devices  160 us (75%)
  between operations  13.5 us (6%)
  matrix products  13.4 us (6%)
  loops' own time  10.4 us (5%)
  local copies, waits for them, and re-layouts  7.58 us (4%)
  starting transfers between devices  5.56 us (3%)
  other arithmetic  2.93 us (1%)
    psum x1, waiting for transfers between devices, per_device(): summed = lax.psum(accumulated, 'op')  156 us
    dot_general x8, matrix products, add_term(): jnp.einsum('vbij,blj->vbil', half_product, right_block, preferred_element...  13.4 us
    another operation x1, loops' own time, per_device(): lax.scan(add_term, initial, (left_ops, right_ops, term_shifts))  10.4 us
    dynamic_slice x8, local copies, waits for them, and re-layouts, per_device(): lax.scan(add_term, initial, (left_ops, right_ops, term_shifts))  5.2 us
  transfers between devices with their start and end apart: 3, of which 3 were waited for; matrix products, arithmetic and copies ran while one was open for 0% of the time, Pallas kernels for 0%

commit v1 on v0

--- a/solution.py
+++ b/solution.py
@@ -48,7 +48,12 @@
     op_count = lax.axis_size("op")
     share_rows = block_order // op_count
     first_row = lax.axis_index("op") * share_rows
-    summed = lax.psum(accumulated, "op")
+
+    def carry_table(s0):
+        x_new = lax.all_gather(s0, "op").sum(axis=0)
+        return x_new
+
+    summed = carry_table(accumulated)
     own_share = lax.dynamic_slice_in_dim(summed, first_row, share_rows, 2)
     live_share = lax.dynamic_slice_in_dim(live_mask, first_row, share_rows, 1)
     return jnp.where(live_share[None], own_share, jnp.zeros((), own_share.dtype))

time: 214 us -> 265 us (1.24)
  the two profiles are of different devices: /device:TPU:2 before, /device:TPU:1 now
where the time goes in v1:
time: 265 us; the launch traced here: 264 us
  waiting for transfers between devices  201 us (76%)
  between operations  13.5 us (5%)
  matrix products  13.4 us (5%)
  starting transfers between devices  10.1 us (4%)
  loops' own time  9.99 us (4%)
  other arithmetic  8.66 us (3%)
  local copies, waits for them, and re-layouts  8.11 us (3%)
    all_gather x1, waiting for transfers between devices, carry_table(): x_new = lax.all_gather(s0, 'op').sum(axis=0)  198 us
    dot_general x8, matrix products, add_term(): jnp.einsum('vbij,blj->vbil', half_product, right_block, preferred_element...  13.4 us
    another operation x1, loops' own time, per_device(): lax.scan(add_term, initial, (left_ops, right_ops, term_shifts))  9.99 us
    reduce_sum x1, other arithmetic, carry_table(): x_new = lax.all_gather(s0, 'op').sum(axis=0)  6.99 us
    ppermute x1, starting transfers between devices, extended(): lax.ppermute(head, axis, [((i + 1) % count, i) for i in range(ends)])  5.55 us
  transfers between devices with their start and end apart: 3, of which 2 were waited for; matrix products, arithmetic and copies ran while one was open for 0% of the time, Pallas kernels for 0%

profile of v1, /device:TPU:1, one launch (start us, length us, event | category | flops | bytes accessed | tf_op | source)
XLA Modules:
  0.0 264.2 jit_solution(16366737950591451829)
XLA Ops:
  6.5 0.0 all-gather.3.cloned.1.call-start
  6.5 1.0 slice_reduce_fusion.1
  7.5 0.1 iota_compare_fusion
  7.6 0.1 broadcast_and_fusion
  7.7 0.3 copy.6
  8.0 0.0 copy-start.1
  8.0 1.1 broadcast_select_fusion
  9.2 4.5 %collective-permute-start = (bf16[2,1,256,256]{3,2,1,0:T(8,128)(2,1)S(1)}, bf16[2,1,256,256]{3,2,1,0:T(8,128)(2,1)S(1)}, u32[]{:S(2)}, u32[]{:S(2)}) collective-permute-start(bf16[2,1,256,256]{3,2,1,0:T(8,128)(2,1)S(1)} %get-tuple-element.118), channel_id=1, source_target_pairs={{0,1},{1,2},{2,3},{3,4},{4,5},{5,6},{6,7},{7,8},{8,9},{9,10},{10,1... | collective-permute-start | bytes 786440 | tf_op jit(solution)/shard_map/ppermute | solution.py:15
  13.7 5.6 %collective-permute-start.1 = (bf16[2,1,256,256]{3,2,1,0:T(8,128)(2,1)S(1)}, bf16[2,1,256,256]{3,2,1,0:T(8,128)(2,1)S(1)}, u32[]{:S(2)}, u32[]{:S(2)}) collective-permute-start(bf16[2,1,256,256]{3,2,1,0:T(8,128)(2,1)S(1)} %get-tuple-element.119), channel_id=1, source_target_pairs={{1,0},{2,1},{3,2},{4,3},{5,4},{6,5},{7,6},{8,7},{9,8},{10,9},{11,1... | collective-permute-start | bytes 786440 | tf_op jit(solution)/shard_map/ppermute | solution.py:17
  19.2 0.0 collective-permute-done
  19.3 2.1 collective-permute-done.1
  21.4 0.1 pad_maximum_fusion
  21.5 0.0 copy-done.1
  21.5 28.4 %while.13 = (s32[]{:T(128)}, f32[2,2,256,256]{2,3,0,1:T(8,128)S(1)}, bf16[8,2,256,256]{3,2,1,0:T(8,128)(2,1)}, s32[8]{0:T(128)S(1)}, bf16[2,4,256,256]{3,2,1,0:T...) while((s32[]{:T(128)}, ...), condition=%wide.region_1.2_spmd.clone, body=%wide.region_0.1_spmd.clone.sunk | while | flops 269221888 | bytes 3147952 | solution.py:47
  21.5 0.6 dynamic_slice.60
  23.4 1.7 fusion.20
  25.1 0.6 dynamic_slice.60
  26.9 1.7 fusion.20
  28.6 0.6 dynamic_slice.60
  30.4 1.7 fusion.20
  32.1 0.6 dynamic_slice.60
  34.0 1.7 fusion.20
  35.7 0.6 dynamic_slice.60
  37.5 1.7 fusion.20
  39.2 0.6 dynamic_slice.60
  41.1 1.7 fusion.20
  42.8 0.6 dynamic_slice.60
  44.6 1.7 fusion.20
  46.3 0.6 dynamic_slice.60
  48.2 1.7 fusion.20
  49.9 0.0 copy-start
  49.9 1.0 copy-done
  50.8 0.0 all-gather.3.cloned.1.call-update
  50.9 0.1 constant_dynamic-slice_fusion.1
  51.0 198.4 %all-gather.3.cloned.1.call-done = f32[32,2,256,256]{2,3,0,1:T(8,128)} async-done(((f32[2,2,256,256]{2,3,0,1:T(8,128)}), f32[32,2,256,256]{2,3,0,1:T(8,128)}) %all-gather.3.cloned.1.call-update) | async-done | bytes 16777232 | tf_op jit(solution)/shard_map/all_gather | solution.py:53
  249.4 7.0 %reduce_sum.9 = f32[2,2,256,256]{2,3,0,1:T(8,128)S(1)} reduce(f32[16,2,2,256,256]{3,4,1,0,2:T(8,128)} %bitcast.36, f32[]{:T(128)} %constant.42.clone.1), dimensions={0}, to_apply=%region_2.3 | reduce | flops 3932160 | bytes 17825796 | tf_op jit(solution)/shard_map/reduce_sum | solution.py:53
  256.4 0.2 dynamic-slice_select_fusion
  256.6 0.8 copy.7
  (2 shorter events, 0.0 us)
Async XLA Ops:
  6.5 242.9 %all-gather.3.cloned.1.call-start = ((), (), s32[]{:S(2)}) async-start(), calls=%async_computation | async-start | bytes 17825792 | tf_op jit(solution)/shard_map/all_gather | solution.py:53
  8.0 13.5 %copy-start.1 = (s32[8]{0:T(128)S(1)}, s32[8]{0:T(128)}, u32[]{:S(2)}) copy-start(s32[8]{0:T(128)} %param.11) | copy-start | bytes 100
  9.2 10.1 %collective-permute-start = (bf16[2,1,256,256]{3,2,1,0:T(8,128)(2,1)S(1)}, bf16[2,1,256,256]{3,2,1,0:T(8,128)(2,1)S(1)}, u32[]{:S(2)}, u32[]{:S(2)}) collective-permute-start(bf16[2,1,256,256]{3,2,1,0:T(8,128)(2,1)S(1)} %get-tuple-element.118), channel_id=1, source_target_pairs={{0,1},{1,2},{2,3},{3,4},{4,5},{5,6},{6,7},{7,8},{8,9},{9,10},{10,1... | collective-permute-start | bytes 786440 | tf_op jit(solution)/shard_map/ppermute | solution.py:15
  13.7 7.7 %collective-permute-start.1 = (bf16[2,1,256,256]{3,2,1,0:T(8,128)(2,1)S(1)}, bf16[2,1,256,256]{3,2,1,0:T(8,128)(2,1)S(1)}, u32[]{:S(2)}, u32[]{:S(2)}) collective-permute-start(bf16[2,1,256,256]{3,2,1,0:T(8,128)(2,1)S(1)} %get-tuple-element.119), channel_id=1, source_target_pairs={{1,0},{2,1},{3,2},{4,3},{5,4},{6,5},{7,6},{8,7},{9,8},{10,9},{11,1... | collective-permute-start | bytes 786440 | tf_op jit(solution)/shard_map/ppermute | solution.py:17
  49.9 1.0 copy-start
Sparse Core Ops, SparseCore 0:
  51.0 198.3 all-gather.2
